TPU v7x, 128 devices: a whole 4x4x4 slice. The times are simulated.
128 devices in a mesh: scen: 8 (over y, x_lo), gx: 4 (over x_hi, core), gy: 4 (over z).
Axes of the slice: x: 4 (x_hi: 2, x_lo: 2; x = x_hi * 2 + x_lo), y: 4, z: 4, core: 2. Of those that a mesh axis runs over, the one named last changes fastest.
Arguments:
- source: float32 [8, 32, 1024, 1024], P('scen', None, 'gx', 'gy'), may hold values from 0.2 to 3
- obstacle: int32 [32, 1024, 1024], P(None, 'gx', 'gy'), may hold values 0 or 1
- sector: int32 [8], P('scen'), may hold values from 0 to 15
- freq_class: int32 [8], P('scen'), may hold values from 0 to 4
Outputs:
- risk: float32 [16, 1024, 1024], P('scen', 'gx', 'gy')
All inputs are finite; a program needn't handle non-finite values. No bound on the sum of `obstacle` on one device may be relied on, other than what follows from the above.
Results may differ from a plain program's by a relative error of at most 0.00002.
Values sent between devices are 32-bit elements; how exact they have to be, the bound alone decides.
No kernel may reach another device: no remote copies, remote signals or barrier semaphores. Data moves between devices by JAX's collectives and lax.ppermute only.
A program may use at most 256 MiB of HBM per device.

v0:
```python
import math
import jax
import jax.numpy as jnp
from jax import lax
from jax.sharding import PartitionSpec as P

STEPS = 4
RZ = 16
wind_speed = 0.4
diffusion = 0.05
settling = 0.1
probit_a = 3.0
probit_b = 1.0
load_eps = 0.01
freq_rate = 0.7


def with_halo(block, sides, width):
    for axis, dim in sides:
        count = lax.axis_size(axis)
        forward = [(i, i + 1) for i in range(count - 1)]
        backward = [(target, source) for source, target in forward]
        low = lax.ppermute(
            lax.slice_in_dim(block, block.shape[dim] - width, None, axis=dim), axis, forward
        )
        high = lax.ppermute(lax.slice_in_dim(block, 0, width, axis=dim), axis, backward)
        block = jnp.concatenate([low, block, high], axis=dim)
    return block


def wind_components(sector_id):
    heading = sector_id.astype(jnp.float32) * (2.0 * math.pi / 16.0)
    return (wind_speed * jnp.cos(heading), wind_speed * jnp.sin(heading))


def advance(padded, open_cells, courant_x, courant_y):
    centre = padded[:, 1:-1, 1:-1]
    west_side = padded[:, :-2, 1:-1]
    east_side = padded[:, 2:, 1:-1]
    south_side = padded[:, 1:-1, :-2]
    north_side = padded[:, 1:-1, 2:]
    zero_plane = jnp.zeros_like(centre[:1])
    upper_cell = jnp.concatenate([centre[1:], zero_plane], 0)
    lower_cell = jnp.concatenate([centre[:1], centre[:-1]], 0)
    falling = jnp.concatenate([zero_plane, centre[1:]], 0)
    advect = jnp.maximum(courant_x, 0.0) * (centre - west_side) + jnp.minimum(courant_x, 0.0) * (
        east_side - centre
    )
    advect = (
        advect
        + jnp.maximum(courant_y, 0.0) * (centre - south_side)
        + jnp.minimum(courant_y, 0.0) * (north_side - centre)
    )
    spread = (
        west_side + east_side + south_side + north_side + upper_cell + lower_cell - 6.0 * centre
    )
    return (centre - advect + diffusion * spread + settling * (upper_cell - falling)) * open_cells


def lethality(toxic_load):
    probit = probit_a + probit_b * jnp.log(toxic_load + load_eps)
    return 0.5 * (1.0 + lax.erf((probit - 5.0) / math.sqrt(2.0)))


def on_device(source, obstacle, sector, freq_class):
    open_cells = (1 - obstacle).astype(jnp.float32)
    courant_x, courant_y = wind_components(sector[0])
    weight = jnp.exp(-freq_rate * freq_class[0].astype(jnp.float32))
    current = source[0] * open_cells
    toxic_load = jnp.zeros_like(current)
    for step_index in range(STEPS):
        padded = with_halo(current, (("gx", 1), ("gy", 2)), 1)
        current = advance(padded, open_cells, courant_x, courant_y)
        toxic_load = toxic_load + current * current
    weighted = weight * lethality(toxic_load[:RZ])
    summed = lax.psum(weighted, "scen")
    share = RZ // lax.axis_size("scen")
    return lax.dynamic_slice_in_dim(summed, lax.axis_index("scen") * share, share, 0)


def solution(mesh):
    in_specs = (P("scen", None, "gx", "gy"), P(None, "gx", "gy"), P("scen"), P("scen"))
    out_specs = P("scen", "gx", "gy")
    return jax.shard_map(
        on_device, mesh=mesh, in_specs=in_specs, out_specs=out_specs, check_vma=False
    )
```

profile of v0, /device:TPU:1, one launch (start us, length us, event | category | flops | bytes accessed | tf_op | source)
XLA Modules:
  0.0 627.8 jit_solution(8884289977543023363)
XLA Ops:
  6.5 16.5 %bitcast_multiply_fusion = f32[32,256,256]{2,0,1:T(8,128)S(1)} fusion(f32[1,32,256,256]{3,2,1,0:T(8,128)} %param.4, s32[32,256,256]{2,1,0:T(8,128)} %param.5), kind=kLoop, calls=%fused_computation.103 | loop fusion | flops 6291456 | bytes 25165824 | tf_op jit(solution)/shard_map/mul | solution.py:69
  23.0 6.0 collective-permute-start
  31.0 4.8 collective-permute-done.1
  36.7 5.0 fusion.83
  54.2 13.4 %fusion.90 = (f32[31,256,256]{2,0,1:T(8,128)}, f32[31,256,256]{2,0,1:T(8,128)}) fusion(f32[32,256,256]{2,0,1:T(8,128)} %copy-done), kind=kLoop, calls=%fused_computation.136 | loop fusion | bytes 32505856 | tf_op jit(solution)/shard_map/slice | solution.py:43
  78.0 39.9 %fusion.59 = f32[32,256,256]{2,0,1:T(8,128)} fusion(f32[32,1,256]{2,0,1:T(8,128)S(1)} %collective-permute-done.1, f32[32,256,256]{2,0,1:T(8,128)} %copy-done, f32[32,1,256]{2,0,1:T(8,128)S(1)} %collective-permute-done, f32[31,256,256]{2,0,1:T(8,128)} %get-tuple-element.26, f32[1,256,256]{2,0,1:T(1,128)S(1)} %slice.205, ...), kind=kLoop, calls=%fused_computation.94 | loop fusion | flops 75497472 | bytes 41812496 | tf_op jit(solution)/shard_map/mul | solution.py:57
  123.0 4.6 collective-permute-done.5
  131.6 4.8 fusion.82
  140.2 4.7 collective-permute-start.6
  149.9 13.5 %fusion.88 = (f32[31,256,256]{2,0,1:T(8,128)}, f32[31,256,256]{2,0,1:T(8,128)}) fusion(f32[32,256,256]{2,0,1:T(8,128)} %fusion.59), kind=kLoop, calls=%fused_computation.134 | loop fusion | bytes 32505856 | tf_op jit(solution)/shard_map/slice | solution.py:43
  172.9 39.3 %fusion.41 = f32[32,256,256]{2,0,1:T(8,128)} fusion(f32[32,1,256]{2,0,1:T(8,128)S(1)} %collective-permute-done.5, f32[32,256,256]{2,0,1:T(8,128)} %fusion.59, f32[32,1,256]{2,0,1:T(8,128)S(1)} %collective-permute-done.4, f32[31,256,256]{2,0,1:T(8,128)} %get-tuple-element.22, f32[1,256,256]{2,0,1:T(1,128)S(1)} %slice.212, ...), kind=kLoop, calls=%fused_computation.68 | loop fusion | flops 75497472 | bytes 41812496 | tf_op jit(solution)/shard_map/mul | solution.py:57
  217.5 4.4 collective-permute-done.9
  225.9 4.8 fusion.81
  234.5 4.3 collective-permute-start.10
  243.8 13.4 %fusion.86 = (f32[31,256,256]{2,0,1:T(8,128)}, f32[31,256,256]{2,0,1:T(8,128)}) fusion(f32[32,256,256]{2,0,1:T(8,128)} %fusion.41), kind=kLoop, calls=%fused_computation.132 | loop fusion | bytes 32505856 | tf_op jit(solution)/shard_map/slice | solution.py:43
  266.6 40.3 %fusion.23 = f32[32,256,256]{2,0,1:T(8,128)} fusion(f32[32,1,256]{2,0,1:T(8,128)S(1)} %collective-permute-done.9, f32[32,256,256]{2,0,1:T(8,128)} %fusion.41, f32[32,1,256]{2,0,1:T(8,128)S(1)} %collective-permute-done.8, f32[31,256,256]{2,0,1:T(8,128)} %get-tuple-element.18, f32[1,256,256]{2,0,1:T(1,128)S(1)} %slice.219, ...), kind=kLoop, calls=%fused_computation.42 | loop fusion | flops 75497472 | bytes 41812496 | tf_op jit(solution)/shard_map/mul | solution.py:57
  312.6 11.7 %fusion.67 = f32[32,256,256]{2,0,1:T(8,128)} fusion(s32[32,256,256]{2,1,0:T(8,128)} %param.5), kind=kLoop, calls=%fused_computation.105 | loop fusion | flops 4194304 | bytes 16777216 | tf_op jit(solution)/shard_map/convert_element_type | solution.py:66
  326.9 4.9 fusion.80
  335.5 4.2 collective-permute-start.14
  345.0 13.4 %fusion.84 = (f32[31,256,256]{2,0,1:T(8,128)}, f32[31,256,256]{2,0,1:T(8,128)}) fusion(f32[32,256,256]{2,0,1:T(8,128)} %fusion.23), kind=kLoop, calls=%fused_computation.130 | loop fusion | bytes 32505856 | tf_op jit(solution)/shard_map/slice | solution.py:44
  367.9 23.8 %fusion.10 = f32[32,256,256]{2,0,1:T(8,128)} fusion(f32[32,256,256]{2,0,1:T(8,128)} %fusion.23, f32[32,1,256]{2,0,1:T(8,128)S(1)} %collective-permute-done.13, f32[32,1,256]{2,0,1:T(8,128)S(1)} %collective-permute-done.12, f32[32,258,1]{2,0,1:T(8,128)} %copy.23, f32[32,258,1]{2,0,1:T(8,128)} %copy.25, f32[]{:T(128)} %bitcast.4, f32[]{:T(128)} %bitcast.3, ...), kind=kLoop, calls=%fused_computation.21 | loop fusion | flops 39845888 | bytes 16908816 | tf_op jit(solution)/shard_map/add | solution.py:50
  391.8 27.2 %fusion.6 = f32[32,256,256]{2,0,1:T(8,128)} fusion(f32[32,1,256]{2,0,1:T(8,128)S(1)} %collective-permute-done.13, f32[32,256,256]{2,0,1:T(8,128)} %fusion.23, f32[32,1,256]{2,0,1:T(8,128)S(1)} %collective-permute-done.12, f32[31,256,256]{2,0,1:T(8,128)} %get-tuple-element.13, f32[1,256,256]{2,0,1:T(1,128)S(1)} %slice.226, ...), kind=kLoop, calls=%fused_computation.17 | loop fusion | flops 33554432 | bytes 33423872 | tf_op jit(solution)/shard_map/sub | solution.py:55
  419.1 13.3 %add_multiply_fusion = f32[16,256,256]{2,0,1:T(8,128)} fusion(f32[32,256,256]{2,0,1:T(8,128)} %fusion.67, f32[31,256,256]{2,0,1:T(8,128)} %get-tuple-element.14, f32[32,256,256]{2,0,1:T(8,128)} %fusion.6, f32[32,256,256]{2,0,1:T(8,128)} %fusion.10, f32[32,256,256]{2,0,1:T(8,128)S(1)} %bitcast.10, f32[32,256,256]{2,0,1:T(8,128)} %fusion.41, ...), kind=kLoop, calls=%fused_computation.124 | loop fusion | flops 19922944 | bytes 37486596 | tf_op jit(solution)/shard_map/mul | solution.py:75
  432.4 185.5 %all-reduce.10.cloned.1.call-done = f32[16,256,256]{2,0,1:T(8,128)} async-done(((f32[16,256,256]{2,0,1:T(8,128)}), f32[16,256,256]{2,0,1:T(8,128)}) %all-reduce.10.cloned.1.call-update) | async-done | bytes 4194320 | tf_op jit(solution)/shard_map/psum | solution.py:76
  (74 shorter events, 108.2 us)
Async XLA Ops:
  6.5 611.4 %all-reduce.10.cloned.1.call-start = ((), (), s32[]{:S(2)}) async-start(), calls=%async_computation | async-start | bytes 8388608 | tf_op jit(solution)/shard_map/psum | solution.py:76
  23.0 12.8 %copy-start = (f32[32,256,256]{2,0,1:T(8,128)}, f32[32,256,256]{2,0,1:T(8,128)S(1)}, u32[]{:S(2)}) copy-start(f32[32,256,256]{2,0,1:T(8,128)S(1)} %bitcast_multiply_fusion) | copy-start | bytes 25165828
  23.0 8.0 %collective-permute-start = (f32[32,1,256]{2,0,1:T(8,128)S(1)}, f32[32,1,256]{2,0,1:T(8,128)S(1)}, u32[]{:S(2)}, u32[]{:S(2)}) collective-permute-start(f32[32,1,256]{2,0,1:T(8,128)S(1)} %get-tuple-element.27), channel_id=1, source_target_pairs={{0,4},{4,8},{8,12},{1,5},{5,9},{9,13},{2,6},{6,10},{10,14},{3,7},{... | collective-permute-start | bytes 98312 | tf_op jit(solution)/shard_map/ppermute | solution.py:23
  29.1 6.7 %collective-permute-start.1 = (f32[32,1,256]{2,0,1:T(8,128)S(1)}, f32[32,1,256]{2,0,1:T(8,128)S(1)}, u32[]{:S(2)}, u32[]{:S(2)}) collective-permute-start(f32[32,1,256]{2,0,1:T(8,128)S(1)} %get-tuple-element.28), channel_id=1, source_target_pairs={{4,0},{8,4},{12,8},{5,1},{9,5},{13,9},{6,2},{10,6},{14,10},{7,3},{... | collective-permute-start | bytes 98312 | tf_op jit(solution)/shard_map/ppermute | solution.py:26
  45.4 24.7 %collective-permute-start.2 = (f32[32,258,1]{1,0,2:T(8,128)S(1)}, f32[32,258,1]{1,0,2:T(8,128)S(1)}, u32[]{:S(2)}, u32[]{:S(2)}) collective-permute-start(f32[32,258,1]{1,0,2:T(8,128)S(1)} %copy.10), channel_id=1, source_target_pairs={{0,1},{1,2},{2,3},{4,5},{5,6},{6,7},{8,9},{9,10},{10,11},{12,13},{... | collective-permute-start | bytes 99080 | tf_op jit(solution)/shard_map/ppermute | solution.py:23
  52.7 21.4 %collective-permute-start.3 = (f32[32,258,1]{1,0,2:T(8,128)S(1)}, f32[32,258,1]{1,0,2:T(8,128)S(1)}, u32[]{:S(2)}, u32[]{:S(2)}) collective-permute-start(f32[32,258,1]{1,0,2:T(8,128)S(1)} %copy.12), channel_id=1, source_target_pairs={{1,0},{2,1},{3,2},{5,4},{6,5},{7,6},{9,8},{10,9},{11,10},{13,12},{... | collective-permute-start | bytes 99080 | tf_op jit(solution)/shard_map/ppermute | solution.py:26
  118.7 4.3 collective-permute-start.4
  120.9 6.7 %collective-permute-start.5 = (f32[32,1,256]{2,0,1:T(8,128)S(1)}, f32[32,1,256]{2,0,1:T(8,128)S(1)}, u32[]{:S(2)}, u32[]{:S(2)}) collective-permute-start(f32[32,1,256]{2,0,1:T(8,128)S(1)} %get-tuple-element.24), channel_id=1, source_target_pairs={{4,0},{8,4},{12,8},{5,1},{9,5},{13,9},{6,2},{10,6},{14,10},{7,3},{... | collective-permute-start | bytes 98312 | tf_op jit(solution)/shard_map/ppermute | solution.py:26
  140.2 24.9 %collective-permute-start.6 = (f32[32,258,1]{1,0,2:T(8,128)S(1)}, f32[32,258,1]{1,0,2:T(8,128)S(1)}, u32[]{:S(2)}, u32[]{:S(2)}) collective-permute-start(f32[32,258,1]{1,0,2:T(8,128)S(1)} %copy.14), channel_id=1, source_target_pairs={{0,1},{1,2},{2,3},{4,5},{5,6},{6,7},{8,9},{9,10},{10,11},{12,13},{... | collective-permute-start | bytes 99080 | tf_op jit(solution)/shard_map/ppermute | solution.py:23
  148.6 20.4 %collective-permute-start.7 = (f32[32,258,1]{1,0,2:T(8,128)S(1)}, f32[32,258,1]{1,0,2:T(8,128)S(1)}, u32[]{:S(2)}, u32[]{:S(2)}) collective-permute-start(f32[32,258,1]{1,0,2:T(8,128)S(1)} %copy.16), channel_id=1, source_target_pairs={{1,0},{2,1},{3,2},{5,4},{6,5},{7,6},{9,8},{10,9},{11,10},{13,12},{... | collective-permute-start | bytes 99080 | tf_op jit(solution)/shard_map/ppermute | solution.py:26
  213.0 4.5 collective-permute-start.8
  215.2 6.7 %collective-permute-start.9 = (f32[32,1,256]{2,0,1:T(8,128)S(1)}, f32[32,1,256]{2,0,1:T(8,128)S(1)}, u32[]{:S(2)}, u32[]{:S(2)}) collective-permute-start(f32[32,1,256]{2,0,1:T(8,128)S(1)} %get-tuple-element.20), channel_id=1, source_target_pairs={{4,0},{8,4},{12,8},{5,1},{9,5},{13,9},{6,2},{10,6},{14,10},{7,3},{... | collective-permute-start | bytes 98312 | tf_op jit(solution)/shard_map/ppermute | solution.py:26
  234.5 24.4 %collective-permute-start.10 = (f32[32,258,1]{1,0,2:T(8,128)S(1)}, f32[32,258,1]{1,0,2:T(8,128)S(1)}, u32[]{:S(2)}, u32[]{:S(2)}) collective-permute-start(f32[32,258,1]{1,0,2:T(8,128)S(1)} %copy.18), channel_id=1, source_target_pairs={{0,1},{1,2},{2,3},{4,5},{5,6},{6,7},{8,9},{9,10},{10,11},{12,13},{... | collective-permute-start | bytes 99080 | tf_op jit(solution)/shard_map/ppermute | solution.py:23
  242.5 20.2 %collective-permute-start.11 = (f32[32,258,1]{1,0,2:T(8,128)S(1)}, f32[32,258,1]{1,0,2:T(8,128)S(1)}, u32[]{:S(2)}, u32[]{:S(2)}) collective-permute-start(f32[32,258,1]{1,0,2:T(8,128)S(1)} %copy.20), channel_id=1, source_target_pairs={{1,0},{2,1},{3,2},{5,4},{6,5},{7,6},{9,8},{10,9},{11,10},{13,12},{... | collective-permute-start | bytes 99080 | tf_op jit(solution)/shard_map/ppermute | solution.py:26
  307.7 17.4 %collective-permute-start.12 = (f32[32,1,256]{2,0,1:T(8,128)S(1)}, f32[32,1,256]{2,0,1:T(8,128)S(1)}, u32[]{:S(2)}, u32[]{:S(2)}) collective-permute-start(f32[32,1,256]{2,0,1:T(8,128)S(1)} %get-tuple-element.15), channel_id=1, source_target_pairs={{0,4},{4,8},{8,12},{1,5},{5,9},{9,13},{2,6},{6,10},{10,14},{3,7},{... | collective-permute-start | bytes 98312 | tf_op jit(solution)/shard_map/ppermute | solution.py:23
  309.9 15.2 %slice-start = ((s8[8388608]{0:T(1024)(128)(4,1)}), s8[4194304]{0:T(1024)(128)(4,1)S(1)}, s32[]{:S(2)}) async-start(s8[8388608]{0:T(1024)(128)(4,1)} %bitcast.7), calls=%async_computation.1 | async-start | bytes 8388608
  309.9 15.2 %slice-start.1 = ((s8[8388608]{0:T(1024)(128)(4,1)}), s8[4194304]{0:T(1024)(128)(4,1)S(1)}, s32[]{:S(2)}) async-start(s8[8388608]{0:T(1024)(128)(4,1)} %bitcast.7), calls=%async_computation.2 | async-start | bytes 8388608
  309.9 15.2 %collective-permute-start.13 = (f32[32,1,256]{2,0,1:T(8,128)S(1)}, f32[32,1,256]{2,0,1:T(8,128)S(1)}, u32[]{:S(2)}, u32[]{:S(2)}) collective-permute-start(f32[32,1,256]{2,0,1:T(8,128)S(1)} %get-tuple-element.16), channel_id=1, source_target_pairs={{4,0},{8,4},{12,8},{5,1},{9,5},{13,9},{6,2},{10,6},{14,10},{7,3},{... | collective-permute-start | bytes 98312 | tf_op jit(solution)/shard_map/ppermute | solution.py:26
  335.5 24.7 %collective-permute-start.14 = (f32[32,258,1]{1,0,2:T(8,128)S(1)}, f32[32,258,1]{1,0,2:T(8,128)S(1)}, u32[]{:S(2)}, u32[]{:S(2)}) collective-permute-start(f32[32,258,1]{1,0,2:T(8,128)S(1)} %copy.22), channel_id=1, source_target_pairs={{0,1},{1,2},{2,3},{4,5},{5,6},{6,7},{8,9},{9,10},{10,11},{12,13},{... | collective-permute-start | bytes 99080 | tf_op jit(solution)/shard_map/ppermute | solution.py:23
  343.5 20.5 %collective-permute-start.15 = (f32[32,258,1]{1,0,2:T(8,128)S(1)}, f32[32,258,1]{1,0,2:T(8,128)S(1)}, u32[]{:S(2)}, u32[]{:S(2)}) collective-permute-start(f32[32,258,1]{1,0,2:T(8,128)S(1)} %copy.24), channel_id=1, source_target_pairs={{1,0},{2,1},{3,2},{5,4},{6,5},{7,6},{9,8},{10,9},{11,10},{13,12},{... | collective-permute-start | bytes 99080 | tf_op jit(solution)/shard_map/ppermute | solution.py:26
  364.0 27.8 %slice-start.4 = ((s8[4227072]{0:T(1024)(128)(4,1)}), s8[32768]{0:T(1024)(128)(4,1)S(1)}, s32[]{:S(2)}) async-start(s8[4227072]{0:T(1024)(128)(4,1)} %bitcast.11), calls=%async_computation.5 | async-start | bytes 65536
  367.9 23.8 %slice-start.5 = ((s8[4227072]{0:T(1024)(128)(4,1)}), s8[4194304]{0:T(1024)(128)(4,1)S(1)}, s32[]{:S(2)}) async-start(s8[4227072]{0:T(1024)(128)(4,1)} %bitcast.11), calls=%async_computation.6 | async-start | bytes 8388608
  367.9 51.1 %slice-start.2 = ((s8[8388608]{0:T(1024)(128)(4,1)}), s8[4194304]{0:T(1024)(128)(4,1)S(1)}, s32[]{:S(2)}) async-start(s8[8388608]{0:T(1024)(128)(4,1)} %bitcast.9), calls=%async_computation.3 | async-start | bytes 8388608
  391.8 27.3 %slice-start.3 = ((s8[8388608]{0:T(1024)(128)(4,1)}), s8[4194304]{0:T(1024)(128)(4,1)S(1)}, s32[]{:S(2)}) async-start(s8[8388608]{0:T(1024)(128)(4,1)} %bitcast.9), calls=%async_computation.4 | async-start | bytes 8388608
Sparse Core Ops, SparseCore 0:
  432.5 185.3 all-reduce.9
where the time goes:
time: 637 us; the launch traced here: 628 us
  other arithmetic  223 us (35%)
  waiting for transfers between devices  199 us (31%)
  local copies, waits for them, and re-layouts  146 us (23%)
  starting transfers between devices  44 us (7%)
  between operations  15.8 us (2%)
    psum x1, waiting for transfers between devices, on_device(): summed = lax.psum(weighted, 'scen')  186 us
    mul x3, other arithmetic, advance(): (centre - advect + diffusion * spread + settling * (upper_cell - falling)...  120 us
    slice x3, local copies, waits for them, and re-layouts, advance(): upper_cell = jnp.concatenate([centre[1:], zero_plane], 0)  40.2 us
    slice x11, local copies, waits for them, and re-layouts, with_halo(): lax.slice_in_dim(block, block.shape[dim] - width, None, axis=dim)  31.9 us
    ppermute x8, starting transfers between devices, with_halo(): lax.ppermute(lax.slice_in_dim(block, block.shape[dim] - width, None, axis...  29.2 us
    sub x1, other arithmetic, advance(): west_side + east_side + south_side + north_side + upper_cell + lower_cell  27.2 us
    add x1, other arithmetic, advance(): advect + jnp.maximum(courant_y, 0.0) * (centre - south_side)  23.8 us
    slice x5, local copies, waits for them, and re-layouts, advance(): lower_cell = jnp.concatenate([centre[:1], centre[:-1]], 0)  20.3 us
  transfers between devices with their start and end apart: 17, of which 4 were waited for; matrix products, arithmetic and copies ran while one was open for 16% of the time, Pallas kernels for 0%

commit v1 on v0

--- a/solution.py
+++ b/solution.py
@@ -73,7 +73,7 @@
         current = advance(padded, open_cells, courant_x, courant_y)
         toxic_load = toxic_load + current * current
     weighted = weight * lethality(toxic_load[:RZ])
-    summed = lax.psum(weighted, "scen")
+    summed = jnp.sum(lax.all_gather(weighted, "scen"), axis=0)
     share = RZ // lax.axis_size("scen")
     return lax.dynamic_slice_in_dim(summed, lax.axis_index("scen") * share, share, 0)
 

time: 637 us -> 1110 us (1.74)
  waiting for transfers between devices: 199 us -> 657 us
  other arithmetic: 223 us -> 235 us
    all_gather x0 -> x1, waiting for transfers between devices: none -> 643 us  [on_device(): summed = jnp.sum(lax.all_gather(weighted, 'scen'), axis=0)]
    psum x1 -> x0, waiting for transfers between devices: 186 us -> none  [on_device(): summed = lax.psum(weighted, 'scen')]
    reduce_sum x0 -> x1, other arithmetic: none -> 14.4 us  [on_device(): summed = jnp.sum(lax.all_gather(weighted, 'scen'), axis=0)]
  transfers between devices with their start and end apart: 17 -> 17, of which waited for: 4 -> 4; matrix products, arithmetic and copies ran while one was open for 16% -> 9% of each run, Pallas kernels for 0% -> 0%
where the time goes in v1:
time: 1110 us; the launch traced here: 1100 us
  waiting for transfers between devices  657 us (59%)
  other arithmetic  235 us (21%)
  local copies, waits for them, and re-layouts  150 us (14%)
  starting transfers between devices  44 us (4%)
  between operations  15.8 us (1%)
    all_gather x1, waiting for transfers between devices, on_device(): summed = jnp.sum(lax.all_gather(weighted, 'scen'), axis=0)  643 us
    mul x3, other arithmetic, advance(): (centre - advect + diffusion * spread + settling * (upper_cell - falling)...  120 us
    slice x3, local copies, waits for them, and re-layouts, advance(): upper_cell = jnp.concatenate([centre[1:], zero_plane], 0)  40.2 us
    slice x11, local copies, waits for them, and re-layouts, with_halo(): lax.slice_in_dim(block, block.shape[dim] - width, None, axis=dim)  31.9 us
    ppermute x8, starting transfers between devices, with_halo(): lax.ppermute(lax.slice_in_dim(block, block.shape[dim] - width, None, axis...  29.2 us
    sub x1, other arithmetic, advance(): west_side + east_side + south_side + north_side + upper_cell + lower_cell  27.2 us
    add x1, other arithmetic, advance(): advect + jnp.maximum(courant_y, 0.0) * (centre - south_side)  23.8 us
  transfers between devices with their start and end apart: 17, of which 4 were waited for; matrix products, arithmetic and copies ran while one was open for 9% of the time, Pallas kernels for 0%

profile of v1, /device:TPU:1, one launch (start us, length us, event | category | flops | bytes accessed | tf_op | source)
XLA Modules:
  0.0 1101.8 jit_solution(3567088120577452072)
XLA Ops:
  6.5 16.5 %bitcast_multiply_fusion = f32[32,256,256]{2,0,1:T(8,128)S(1)} fusion(f32[1,32,256,256]{3,2,1,0:T(8,128)} %param.4, s32[32,256,256]{2,1,0:T(8,128)} %param.5), kind=kLoop, calls=%fused_computation.103 | loop fusion | flops 6291456 | bytes 25165824 | tf_op jit(solution)/shard_map/mul | solution.py:69
  23.0 6.0 collective-permute-start
  31.0 4.8 collective-permute-done.1
  36.7 5.0 fusion.83
  54.2 13.4 %fusion.90 = (f32[31,256,256]{2,0,1:T(8,128)}, f32[31,256,256]{2,0,1:T(8,128)}) fusion(f32[32,256,256]{2,0,1:T(8,128)} %copy-done), kind=kLoop, calls=%fused_computation.136 | loop fusion | bytes 32505856 | tf_op jit(solution)/shard_map/slice | solution.py:43
  78.0 39.9 %fusion.59 = f32[32,256,256]{2,0,1:T(8,128)} fusion(f32[32,1,256]{2,0,1:T(8,128)S(1)} %collective-permute-done.1, f32[32,256,256]{2,0,1:T(8,128)} %copy-done, f32[32,1,256]{2,0,1:T(8,128)S(1)} %collective-permute-done, f32[31,256,256]{2,0,1:T(8,128)} %get-tuple-element.26, f32[1,256,256]{2,0,1:T(1,128)S(1)} %slice.205, ...), kind=kLoop, calls=%fused_computation.94 | loop fusion | flops 75497472 | bytes 41812496 | tf_op jit(solution)/shard_map/mul | solution.py:57
  123.0 4.6 collective-permute-done.5
  131.6 4.8 fusion.82
  140.2 4.7 collective-permute-start.6
  149.9 13.5 %fusion.88 = (f32[31,256,256]{2,0,1:T(8,128)}, f32[31,256,256]{2,0,1:T(8,128)}) fusion(f32[32,256,256]{2,0,1:T(8,128)} %fusion.59), kind=kLoop, calls=%fused_computation.134 | loop fusion | bytes 32505856 | tf_op jit(solution)/shard_map/slice | solution.py:43
  172.9 39.3 %fusion.41 = f32[32,256,256]{2,0,1:T(8,128)} fusion(f32[32,1,256]{2,0,1:T(8,128)S(1)} %collective-permute-done.5, f32[32,256,256]{2,0,1:T(8,128)} %fusion.59, f32[32,1,256]{2,0,1:T(8,128)S(1)} %collective-permute-done.4, f32[31,256,256]{2,0,1:T(8,128)} %get-tuple-element.22, f32[1,256,256]{2,0,1:T(1,128)S(1)} %slice.212, ...), kind=kLoop, calls=%fused_computation.68 | loop fusion | flops 75497472 | bytes 41812496 | tf_op jit(solution)/shard_map/mul | solution.py:57
  217.5 4.4 collective-permute-done.9
  225.9 4.8 fusion.81
  243.8 13.4 %fusion.86 = (f32[31,256,256]{2,0,1:T(8,128)}, f32[31,256,256]{2,0,1:T(8,128)}) fusion(f32[32,256,256]{2,0,1:T(8,128)} %fusion.41), kind=kLoop, calls=%fused_computation.132 | loop fusion | bytes 32505856 | tf_op jit(solution)/shard_map/slice | solution.py:43
  266.6 40.3 %fusion.23 = f32[32,256,256]{2,0,1:T(8,128)} fusion(f32[32,1,256]{2,0,1:T(8,128)S(1)} %collective-permute-done.9, f32[32,256,256]{2,0,1:T(8,128)} %fusion.41, f32[32,1,256]{2,0,1:T(8,128)S(1)} %collective-permute-done.8, f32[31,256,256]{2,0,1:T(8,128)} %get-tuple-element.18, f32[1,256,256]{2,0,1:T(1,128)S(1)} %slice.219, ...), kind=kLoop, calls=%fused_computation.42 | loop fusion | flops 75497472 | bytes 41812496 | tf_op jit(solution)/shard_map/mul | solution.py:57
  312.6 11.7 %fusion.67 = f32[32,256,256]{2,0,1:T(8,128)} fusion(s32[32,256,256]{2,1,0:T(8,128)} %param.5), kind=kLoop, calls=%fused_computation.105 | loop fusion | flops 4194304 | bytes 16777216 | tf_op jit(solution)/shard_map/convert_element_type | solution.py:66
  326.9 4.9 fusion.80
  345.0 13.5 %fusion.84 = (f32[31,256,256]{2,0,1:T(8,128)}, f32[31,256,256]{2,0,1:T(8,128)}) fusion(f32[32,256,256]{2,0,1:T(8,128)} %fusion.23), kind=kLoop, calls=%fused_computation.130 | loop fusion | bytes 32505856 | tf_op jit(solution)/shard_map/slice | solution.py:44
  368.0 23.8 %fusion.10 = f32[32,256,256]{2,0,1:T(8,128)} fusion(f32[32,256,256]{2,0,1:T(8,128)} %fusion.23, f32[32,1,256]{2,0,1:T(8,128)S(1)} %collective-permute-done.13, f32[32,1,256]{2,0,1:T(8,128)S(1)} %collective-permute-done.12, f32[32,258,1]{2,0,1:T(8,128)} %copy.23, f32[32,258,1]{2,0,1:T(8,128)} %copy.25, f32[]{:T(128)} %bitcast.4, f32[]{:T(128)} %bitcast.3, ...), kind=kLoop, calls=%fused_computation.21 | loop fusion | flops 39845888 | bytes 16908816 | tf_op jit(solution)/shard_map/add | solution.py:50
  391.8 27.2 %fusion.6 = f32[32,256,256]{2,0,1:T(8,128)} fusion(f32[32,1,256]{2,0,1:T(8,128)S(1)} %collective-permute-done.13, f32[32,256,256]{2,0,1:T(8,128)} %fusion.23, f32[32,1,256]{2,0,1:T(8,128)S(1)} %collective-permute-done.12, f32[31,256,256]{2,0,1:T(8,128)} %get-tuple-element.13, f32[1,256,256]{2,0,1:T(1,128)S(1)} %slice.226, ...), kind=kLoop, calls=%fused_computation.17 | loop fusion | flops 33554432 | bytes 33423872 | tf_op jit(solution)/shard_map/sub | solution.py:55
  419.0 11.5 %add_multiply_fusion = f32[16,256,256]{2,0,1:T(8,128)S(1)} fusion(f32[32,256,256]{2,0,1:T(8,128)} %fusion.67, f32[31,256,256]{2,0,1:T(8,128)} %get-tuple-element.14, f32[32,256,256]{2,0,1:T(8,128)} %fusion.6, f32[32,256,256]{2,0,1:T(8,128)} %fusion.10, f32[32,256,256]{2,0,1:T(8,128)S(1)} %bitcast.11, f32[32,256,256]{2,0,1:T(8,128)} %fusion.41, ...), kind=kLoop, calls=%fused_computation.124 | loop fusion | flops 19922944 | bytes 37486596 | tf_op jit(solution)/shard_map/mul | solution.py:75
  430.5 4.5 copy.26
  435.0 643.2 %all-gather.3.cloned.1.call-done = f32[128,256,256]{2,1,0:T(8,128)} async-done(((f32[16,256,256]{2,1,0:T(8,128)}), f32[128,256,256]{2,1,0:T(8,128)}) %all-gather.3.cloned.1.call-update) | async-done | bytes 33554448 | tf_op jit(solution)/shard_map/all_gather | solution.py:76
  1078.3 14.4 %reduce_sum.9 = f32[16,256,256]{2,1,0:T(8,128)} reduce(f32[8,16,256,256]{3,2,1,0:T(8,128)} %bitcast.14, f32[]{:T(128)} %constant.11.clone.1), dimensions={0}, to_apply=%region_0.0 | reduce | flops 7340032 | bytes 37748740 | tf_op jit(solution)/shard_map/reduce_sum | solution.py:76
  (75 shorter events, 115.9 us)
Async XLA Ops:
  6.5 1071.7 %all-gather.3.cloned.1.call-start = ((), (), s32[]{:S(2)}) async-start(), calls=%async_computation | async-start | bytes 37748736 | tf_op jit(solution)/shard_map/all_gather | solution.py:76
  23.0 12.8 %copy-start = (f32[32,256,256]{2,0,1:T(8,128)}, f32[32,256,256]{2,0,1:T(8,128)S(1)}, u32[]{:S(2)}) copy-start(f32[32,256,256]{2,0,1:T(8,128)S(1)} %bitcast_multiply_fusion) | copy-start | bytes 25165828
  23.0 8.0 collective-permute-start
  29.1 6.7 collective-permute-start.1
  45.4 24.7 %collective-permute-start.2 = (f32[32,258,1]{1,0,2:T(8,128)S(1)}, f32[32,258,1]{1,0,2:T(8,128)S(1)}, u32[]{:S(2)}, u32[]{:S(2)}) collective-permute-start(f32[32,258,1]{1,0,2:T(8,128)S(1)} %copy.10), channel_id=1, source_target_pairs={{0,1},{1,2},{2,3},{4,5},{5,6},{6,7},{8,9},{9,10},{10,11},{12,13},{... | collective-permute-start | bytes 99080 | tf_op jit(solution)/shard_map/ppermute | solution.py:23
  52.7 21.4 %collective-permute-start.3 = (f32[32,258,1]{1,0,2:T(8,128)S(1)}, f32[32,258,1]{1,0,2:T(8,128)S(1)}, u32[]{:S(2)}, u32[]{:S(2)}) collective-permute-start(f32[32,258,1]{1,0,2:T(8,128)S(1)} %copy.12), channel_id=1, source_target_pairs={{1,0},{2,1},{3,2},{5,4},{6,5},{7,6},{9,8},{10,9},{11,10},{13,12},{... | collective-permute-start | bytes 99080 | tf_op jit(solution)/shard_map/ppermute | solution.py:26
  118.7 4.3 collective-permute-start.4
  120.9 6.7 collective-permute-start.5
  140.2 24.9 %collective-permute-start.6 = (f32[32,258,1]{1,0,2:T(8,128)S(1)}, f32[32,258,1]{1,0,2:T(8,128)S(1)}, u32[]{:S(2)}, u32[]{:S(2)}) collective-permute-start(f32[32,258,1]{1,0,2:T(8,128)S(1)} %copy.14), channel_id=1, source_target_pairs={{0,1},{1,2},{2,3},{4,5},{5,6},{6,7},{8,9},{9,10},{10,11},{12,13},{... | collective-permute-start | bytes 99080 | tf_op jit(solution)/shard_map/ppermute | solution.py:23
  148.6 20.4 %collective-permute-start.7 = (f32[32,258,1]{1,0,2:T(8,128)S(1)}, f32[32,258,1]{1,0,2:T(8,128)S(1)}, u32[]{:S(2)}, u32[]{:S(2)}) collective-permute-start(f32[32,258,1]{1,0,2:T(8,128)S(1)} %copy.16), channel_id=1, source_target_pairs={{1,0},{2,1},{3,2},{5,4},{6,5},{7,6},{9,8},{10,9},{11,10},{13,12},{... | collective-permute-start | bytes 99080 | tf_op jit(solution)/shard_map/ppermute | solution.py:26
  213.0 4.5 collective-permute-start.8
  215.2 6.7 collective-permute-start.9
  234.5 24.4 %collective-permute-start.10 = (f32[32,258,1]{1,0,2:T(8,128)S(1)}, f32[32,258,1]{1,0,2:T(8,128)S(1)}, u32[]{:S(2)}, u32[]{:S(2)}) collective-permute-start(f32[32,258,1]{1,0,2:T(8,128)S(1)} %copy.18), channel_id=1, source_target_pairs={{0,1},{1,2},{2,3},{4,5},{5,6},{6,7},{8,9},{9,10},{10,11},{12,13},{... | collective-permute-start | bytes 99080 | tf_op jit(solution)/shard_map/ppermute | solution.py:23
  242.5 20.2 %collective-permute-start.11 = (f32[32,258,1]{1,0,2:T(8,128)S(1)}, f32[32,258,1]{1,0,2:T(8,128)S(1)}, u32[]{:S(2)}, u32[]{:S(2)}) collective-permute-start(f32[32,258,1]{1,0,2:T(8,128)S(1)} %copy.20), channel_id=1, source_target_pairs={{1,0},{2,1},{3,2},{5,4},{6,5},{7,6},{9,8},{10,9},{11,10},{13,12},{... | collective-permute-start | bytes 99080 | tf_op jit(solution)/shard_map/ppermute | solution.py:26
  307.7 17.4 %collective-permute-start.12 = (f32[32,1,256]{2,0,1:T(8,128)S(1)}, f32[32,1,256]{2,0,1:T(8,128)S(1)}, u32[]{:S(2)}, u32[]{:S(2)}) collective-permute-start(f32[32,1,256]{2,0,1:T(8,128)S(1)} %get-tuple-element.15), channel_id=1, source_target_pairs={{0,4},{4,8},{8,12},{1,5},{5,9},{9,13},{2,6},{6,10},{10,14},{3,7},{... | collective-permute-start | bytes 98312 | tf_op jit(solution)/shard_map/ppermute | solution.py:23
  309.9 15.2 %slice-start = ((s8[8388608]{0:T(1024)(128)(4,1)}), s8[4194304]{0:T(1024)(128)(4,1)S(1)}, s32[]{:S(2)}) async-start(s8[8388608]{0:T(1024)(128)(4,1)} %bitcast.8), calls=%async_computation.1 | async-start | bytes 8388608
  309.9 15.2 %slice-start.1 = ((s8[8388608]{0:T(1024)(128)(4,1)}), s8[4194304]{0:T(1024)(128)(4,1)S(1)}, s32[]{:S(2)}) async-start(s8[8388608]{0:T(1024)(128)(4,1)} %bitcast.8), calls=%async_computation.2 | async-start | bytes 8388608
  309.9 15.2 %collective-permute-start.13 = (f32[32,1,256]{2,0,1:T(8,128)S(1)}, f32[32,1,256]{2,0,1:T(8,128)S(1)}, u32[]{:S(2)}, u32[]{:S(2)}) collective-permute-start(f32[32,1,256]{2,0,1:T(8,128)S(1)} %get-tuple-element.16), channel_id=1, source_target_pairs={{4,0},{8,4},{12,8},{5,1},{9,5},{13,9},{6,2},{10,6},{14,10},{7,3},{... | collective-permute-start | bytes 98312 | tf_op jit(solution)/shard_map/ppermute | solution.py:26
  335.5 24.7 %collective-permute-start.14 = (f32[32,258,1]{1,0,2:T(8,128)S(1)}, f32[32,258,1]{1,0,2:T(8,128)S(1)}, u32[]{:S(2)}, u32[]{:S(2)}) collective-permute-start(f32[32,258,1]{1,0,2:T(8,128)S(1)} %copy.22), channel_id=1, source_target_pairs={{0,1},{1,2},{2,3},{4,5},{5,6},{6,7},{8,9},{9,10},{10,11},{12,13},{... | collective-permute-start | bytes 99080 | tf_op jit(solution)/shard_map/ppermute | solution.py:23
  343.5 20.6 %collective-permute-start.15 = (f32[32,258,1]{1,0,2:T(8,128)S(1)}, f32[32,258,1]{1,0,2:T(8,128)S(1)}, u32[]{:S(2)}, u32[]{:S(2)}) collective-permute-start(f32[32,258,1]{1,0,2:T(8,128)S(1)} %copy.24), channel_id=1, source_target_pairs={{1,0},{2,1},{3,2},{5,4},{6,5},{7,6},{9,8},{10,9},{11,10},{13,12},{... | collective-permute-start | bytes 99080 | tf_op jit(solution)/shard_map/ppermute | solution.py:26
  364.0 27.7 %slice-start.4 = ((s8[4227072]{0:T(1024)(128)(4,1)}), s8[32768]{0:T(1024)(128)(4,1)S(1)}, s32[]{:S(2)}) async-start(s8[4227072]{0:T(1024)(128)(4,1)} %bitcast.12), calls=%async_computation.5 | async-start | bytes 65536
  368.0 23.8 %slice-start.5 = ((s8[4227072]{0:T(1024)(128)(4,1)}), s8[4194304]{0:T(1024)(128)(4,1)S(1)}, s32[]{:S(2)}) async-start(s8[4227072]{0:T(1024)(128)(4,1)} %bitcast.12), calls=%async_computation.6 | async-start | bytes 8388608
  368.0 51.0 %slice-start.2 = ((s8[8388608]{0:T(1024)(128)(4,1)}), s8[4194304]{0:T(1024)(128)(4,1)S(1)}, s32[]{:S(2)}) async-start(s8[8388608]{0:T(1024)(128)(4,1)} %bitcast.10), calls=%async_computation.3 | async-start | bytes 8388608
  391.8 27.2 %slice-start.3 = ((s8[8388608]{0:T(1024)(128)(4,1)}), s8[4194304]{0:T(1024)(128)(4,1)S(1)}, s32[]{:S(2)}) async-start(s8[8388608]{0:T(1024)(128)(4,1)} %bitcast.10), calls=%async_computation.4 | async-start | bytes 8388608
Sparse Core Ops, SparseCore 0:
  435.2 643.0 all-gather.2
